TPU v7x, 32 devices: a whole 2x2x4 slice. The times are simulated.
32 devices in a mesh: req: 16 (over z, x, core), kv: 2 (over y).
Axes of the slice: x: 2, y: 2, z: 4, core: 2. Of those that a mesh axis runs over, the one named last changes fastest.
Arguments:
- hidden: bfloat16 [32, 256, 1024], P('req', 'kv'), may hold values from -6 to 6
- queries: bfloat16 [32, 256, 1024], P('req', 'kv'), may hold values from -24 to 24
- span_kv: bfloat16 [32, 256, 8, 128], P('req', 'kv'), may hold values from -48 to 48
- cache: bfloat16 [32, 2048, 8, 128], P('req', 'kv'), may hold values from -48 to 48
- req_order: int32 [32], replicated, may hold values from 0 to 31, each once
- cached_len: int32 [32], replicated, may hold values from 8 to 2048, as said below
- out_weight: bfloat16 [1024, 1024], replicated, may hold values from -0.1875 to 0.1875
- norm_gain: float32 [1024], replicated, may hold values from 0.1 to 1.9
- expert_ids: int32 [8192, 8], P(('req', 'kv')), may hold values from 0 to 15, all different within a row; in each aligned block of 256 rows (0 to 255, 256 to 511, ...) at most 256 rows name the same one
- expert_weights: float32 [8192, 8], P(('req', 'kv')), may hold values from 0.05 to 0.5
- w_experts: bfloat16 [16, 3, 1024, 512], P('req', None, None, 'kv'), may hold values from -0.25 to 0.25
- block_map: int32 [32, 128], P('req'), may hold values from 0 to 4095, as said below
Outputs:
- layer_out: bfloat16 [32, 256, 1024], P('req', 'kv')
- decode_pool: bfloat16 [4096, 8, 16, 128], P('req', 'kv')
Inputs may be any that keep to these rules, and one draw needn't show every extreme that they name: `cached_len`: some request fills its cache. `block_map`: a permutation of the 4096 pool pages; pool page s belongs to req index s // 256; the pages that one kv index holds of the slots of one req index (positions of its cache share) go to every req index equally often. `expert_ids`: in the rows of one device no expert is named more than 256 times.
All inputs are finite; a program needn't handle non-finite values.
Results may differ from a plain program's by a relative error of at most 0.023.
Values may be sent and summed in bfloat16 or wider, within the bound.
No kernel may reach another device: no remote copies, remote signals or barrier semaphores. Data moves between devices by JAX's collectives and lax.ppermute only.
A program may use at most 128 MiB of HBM per device.

v0:
```python
import math
import jax
import jax.numpy as jnp
from jax import lax
from jax.sharding import PartitionSpec as P

BLOCK = 16


def lookup_lengths(req_order, cached_len, count):
    start = lax.axis_index("req") * count
    mine = lax.dynamic_slice_in_dim(req_order, start, count)
    match = mine[:, None] == jnp.arange(cached_len.shape[0], dtype=jnp.int32)[None, :]
    return jnp.sum(jnp.where(match, cached_len[None, :], 0), axis=1)


def score_block(query_rows, cache_rows, span_rows):
    span_count, group_count, width = query_rows.shape
    head_dim = cache_rows.shape[-1] // 2
    per_group = width // head_dim
    query_split = query_rows.reshape(span_count, group_count, per_group, head_dim)
    key_rows = jnp.concatenate([cache_rows[..., :head_dim], span_rows[..., :head_dim]], axis=0)
    value_rows = jnp.concatenate([cache_rows[..., head_dim:], span_rows[..., head_dim:]], axis=0)
    scores = jnp.einsum(
        "igsd,pgd->gsip", query_split, key_rows, preferred_element_type=jnp.float32
    ) * (1.0 / math.sqrt(head_dim))
    return (scores, value_rows)


def soft_weights(scores, allowed, value_rows):
    masked = jnp.where(allowed, scores, -1e30)
    row_max = jnp.max(masked, axis=-1, keepdims=True)
    probability = jnp.where(allowed, jnp.exp(masked - row_max), 0.0)
    prob_sum = jnp.sum(probability, axis=-1)
    weighted = jnp.einsum(
        "gsip,pgd->igsd",
        probability.astype(jnp.bfloat16),
        value_rows,
        preferred_element_type=jnp.float32,
    )
    return (weighted, jnp.transpose(row_max[..., 0], (2, 0, 1)), jnp.transpose(prob_sum, (2, 0, 1)))


def whole_request(operands):
    query_rows, cache_rows, span_rows, length = operands
    scores, value_rows = score_block(query_rows, cache_rows, span_rows)
    cached = cache_rows.shape[0]
    position = jnp.arange(scores.shape[-1])[None, :]
    query_pos = jnp.arange(query_rows.shape[0])[:, None]
    allowed = jnp.where(position < cached, position < length, position - cached <= query_pos)
    weighted, row_max, prob_sum = soft_weights(scores, allowed, value_rows)
    result = weighted / prob_sum[..., None]
    return result.reshape(query_rows.shape).astype(jnp.bfloat16)


def place_pages(page_rows, slot_numbers, slots_dev):
    owner_index = slot_numbers // slots_dev
    arrangement = jnp.argsort(owner_index, stable=True)
    return (page_rows[arrangement], (slot_numbers % slots_dev)[arrangement])


def body(
    hidden,
    queries,
    span_kv,
    cache,
    req_order,
    cached_len,
    out_weight,
    norm_gain,
    expert_ids,
    expert_weights,
    w_experts,
    block_map,
):
    local_reqs, local_tokens, width_model = hidden.shape
    row_count = local_reqs * local_tokens
    req_count = lax.axis_size("req")
    kv_count = lax.axis_size("kv")
    kv_heads = span_kv.shape[2]
    head_pair = span_kv.shape[3]
    group_width = queries.shape[2] // kv_heads
    group_count = kv_heads // kv_count
    slots_dev = local_reqs * block_map.shape[1]
    lengths = lookup_lengths(req_order, cached_len, local_reqs)
    queries_grouped = queries.reshape(local_reqs, local_tokens, kv_heads, group_width)
    cache_heads, span_heads, query_heads = (
        lax.all_to_all(cache, "kv", split_axis=2, concat_axis=1, tiled=True),
        lax.all_to_all(span_kv, "kv", split_axis=2, concat_axis=1, tiled=True),
        lax.all_to_all(queries_grouped, "kv", split_axis=2, concat_axis=1, tiled=True),
    )
    attn_heads = lax.map(whole_request, (query_heads, cache_heads, span_heads, lengths))
    attn = lax.all_to_all(attn_heads, "kv", split_axis=1, concat_axis=2, tiled=True).reshape(
        row_count, kv_heads * group_width
    )
    page_total = block_map.shape[1]
    visible = jnp.arange(cache_heads.shape[1])[None, :] < lengths[:, None]
    visible_cache = jnp.where(visible[:, :, None, None], cache_heads, jnp.zeros((), jnp.bfloat16))
    page_rows = (
        visible_cache.reshape(local_reqs, page_total, BLOCK, group_count, head_pair)
        .transpose(0, 1, 3, 2, 4)
        .reshape(local_reqs * page_total, group_count, BLOCK, head_pair)
    )
    sorted_pages, local_slot = place_pages(page_rows, block_map.reshape(-1), slots_dev)
    per_owner = sorted_pages.shape[0] // req_count
    outgoing = sorted_pages.reshape(req_count, per_owner, group_count, BLOCK, head_pair)
    arrived, where_to = (
        lax.all_to_all(outgoing, "req", split_axis=0, concat_axis=0, tiled=True),
        lax.all_to_all(
            local_slot.reshape(req_count, per_owner), "req", split_axis=0, concat_axis=0, tiled=True
        ),
    )
    decode_pool = (
        jnp.zeros((slots_dev, group_count, BLOCK, head_pair), jnp.bfloat16)
        .at[where_to.reshape(-1)]
        .set(arrived.reshape(-1, group_count, BLOCK, head_pair))
    )
    residual = hidden.reshape(row_count, width_model).astype(jnp.float32) + jnp.dot(
        attn, out_weight, preferred_element_type=jnp.float32
    )
    inverse_rms = lax.rsqrt(jnp.mean(residual * residual, axis=-1, keepdims=True) + 1e-05)
    normed = (residual * inverse_rms * norm_gain).astype(jnp.bfloat16)
    top_count = expert_ids.shape[1]
    exp_dev = w_experts.shape[0]
    experts = exp_dev * req_count
    capacity = min(row_count, 2 * row_count * top_count // experts)
    chosen = expert_ids.reshape(-1)
    onehot = (chosen[:, None] == jnp.arange(experts, dtype=jnp.int32)[None, :]).astype(jnp.int32)
    slot_rank = jnp.sum(onehot * (jnp.cumsum(onehot, axis=0) - 1), axis=1)
    target = chosen * capacity + slot_rank
    source_row = jnp.arange(chosen.shape[0]) // top_count
    buffer = (
        jnp.zeros((experts * capacity, width_model), jnp.bfloat16)
        .at[target]
        .set(normed[source_row])
        .reshape(experts, capacity, width_model)
    )
    full_weights = lax.all_gather(w_experts, "kv", axis=3, tiled=True)
    slot_block = lax.all_to_all(buffer, "req", split_axis=0, concat_axis=0, tiled=True)
    source_count = slot_block.shape[0] // exp_dev
    grouped = slot_block.reshape(source_count, exp_dev, slot_block.shape[1], width_model)
    gate_act = jnp.einsum(
        "sejd,edf->sejf", grouped, full_weights[:, 0], preferred_element_type=jnp.float32
    )
    up_act = jnp.einsum(
        "sejd,edf->sejf", grouped, full_weights[:, 1], preferred_element_type=jnp.float32
    )
    activated = (jax.nn.silu(gate_act) * up_act).astype(jnp.bfloat16)
    expert_out = jnp.einsum(
        "sejf,edf->sejd", activated, full_weights[:, 2], preferred_element_type=jnp.float32
    ).astype(jnp.bfloat16)
    returned = lax.all_to_all(
        expert_out.reshape(slot_block.shape), "req", split_axis=0, concat_axis=0, tiled=True
    )
    picked = returned.reshape(experts * capacity, width_model)[target].reshape(
        row_count, top_count, width_model
    )
    expert_sum = jnp.sum(expert_weights[..., None] * picked.astype(jnp.float32), axis=1)
    layer_out = (
        (residual + expert_sum).astype(jnp.bfloat16).reshape(local_reqs, local_tokens, width_model)
    )
    return (layer_out, decode_pool)


def solution(mesh):
    return jax.shard_map(
        body,
        mesh=mesh,
        in_specs=(
            P("req", "kv", None),
            P("req", "kv", None),
            P("req", "kv", None, None),
            P("req", "kv", None, None),
            P(),
            P(),
            P(),
            P(),
            P(("req", "kv"), None),
            P(("req", "kv"), None),
            P("req", None, None, "kv"),
            P("req", None),
        ),
        out_specs=(P("req", "kv", None), P("req", "kv", None, None)),
        check_vma=False,
    )
```

profile of v0, /device:TPU:11, one launch (start us, length us, event | category | flops | bytes accessed | tf_op | source)
XLA Modules:
  0.0 748.4 jit_solution(12969157909613193286)
XLA Ops:
  7.2 2.1 copy.81
  9.3 3.5 all-to-all-start.1
  14.9 5.2 all-to-all-done.1
  20.1 3.5 all-to-all-start.2
  24.0 5.0 copy.78
  30.1 5.6 all-to-all-start
  35.7 4.5 reduce-window.6
  41.8 3.2 sort.17
  48.8 2.2 all_to_all.74
  52.0 28.7 %all-to-all-done = bf16[2,1024,8,128]{3,1,0,2:T(8,128)(2,1)} async-done(((bf16[2,1024,8,128]{3,1,0,2:T(8,128)(2,1)}), bf16[2,1024,8,128]{3,1,0,2:T(8,128)(2,1)}, u32[]{:S(2)}, u32[]{:S(2)}) %all-to-all-start) | async-done | bytes 4194336 | tf_op jit(solution)/shard_map/all_to_all | solution.py:88
  80.7 4.6 copy.80
  85.3 104.1 %while.12 = (s32[]{:T(128)}, bf16[2,256,4,128]{3,2,0,1:T(4,128)(2,1)}, bf16[2,2048,4,128]{3,1,2,0:T(8,128)(2,1)}, bf16[2,256,4,128]{1,3,2,0:T(8,128)(2,1)}, s32[...) while((s32[]{:T(128)}, bf16[2,256,4,128]{3,2,0,1:T(4,128)(2,1)}, ...), condition=%wide.region_4.5_spmd, body=%wide.region_1.4_spmd.sunk | while | flops 1251877888 | bytes 80653984 | solution.py:92
  85.3 3.0 constant_dynamic-slice_fusion.5
  88.3 4.0 copy.115
  92.3 2.8 fusion.64
  97.6 9.2 %fusion.65 = f32[4,2304,256,2]{2,1,3,0:T(8,128)} fusion(bf16[256,4,2,64]{0,3,2,1:T(8,128)(2,1)S(1)} %bitcast.190, bf16[256,4,64]{0,2,1:T(8,128)(2,1)} %get-tuple-element.183, bf16[2048,4,64]{0,2,1:T(8,128)(2,1)} %get-tuple-element.184), kind=kOutput, calls=%fused_computation.24.clone.1 | convolution fusion | flops 606339072 | bytes 20316160 | tf_op jit(solution)/shard_map/while/body/eval_jaxpr/igsd,pgd->gsip/dot_general | solution.py:24
  108.7 2.7 fusion.66
  111.4 19.4 %fusion.67 = (f32[4,2,256]{2,1,0:T(2,128)S(1)}, bf16[4,2,256,2304]{2,3,1,0:T(8,128)(2,1)}) fusion(f32[4,2304,256,2]{2,1,3,0:T(8,128)} %fusion.65, pred[256,2304]{0,1:T(8,128)(4,1)} %fusion.66), kind=kOutput, calls=%fused_computation.99.clone.1 | output fusion | flops 37751040 | bytes 28909568 | tf_op jit(solution)/shard_map/while/body/eval_jaxpr/sub | solution.py:33
  130.9 5.5 fusion.68
  137.3 3.0 constant_dynamic-slice_fusion.5
  140.4 4.0 copy.115
  144.4 2.8 fusion.64
  149.7 9.2 %fusion.65 = f32[4,2304,256,2]{2,1,3,0:T(8,128)} fusion(bf16[256,4,2,64]{0,3,2,1:T(8,128)(2,1)S(1)} %bitcast.190, bf16[256,4,64]{0,2,1:T(8,128)(2,1)} %get-tuple-element.183, bf16[2048,4,64]{0,2,1:T(8,128)(2,1)} %get-tuple-element.184), kind=kOutput, calls=%fused_computation.24.clone.1 | convolution fusion | flops 606339072 | bytes 20316160 | tf_op jit(solution)/shard_map/while/body/eval_jaxpr/igsd,pgd->gsip/dot_general | solution.py:24
  160.8 2.7 fusion.66
  163.5 19.4 %fusion.67 = (f32[4,2,256]{2,1,0:T(2,128)S(1)}, bf16[4,2,256,2304]{2,3,1,0:T(8,128)(2,1)}) fusion(f32[4,2304,256,2]{2,1,3,0:T(8,128)} %fusion.65, pred[256,2304]{0,1:T(8,128)(4,1)} %fusion.66), kind=kOutput, calls=%fused_computation.99.clone.1 | output fusion | flops 37751040 | bytes 28909568 | tf_op jit(solution)/shard_map/while/body/eval_jaxpr/sub | solution.py:33
  182.9 5.5 fusion.68
  189.4 3.6 all-to-all-start.3
  193.1 1.9 gather_fusion.1
  196.4 2.0 all-to-all-done.3
  198.4 10.7 %all-to-all-start.6 = ((s32[16,1,16]{2,1,0:T(1,128)}), s32[16,1,16]{2,1,0:T(1,128)S(1)}, u32[]{:S(2)}, u32[]{:S(2)}) async-start(s32[16,1,16]{2,1,0:T(1,128)} %all_to_all.84), calls=%async_computation.6 | async-start | bytes 16384 | tf_op jit(solution)/shard_map/all_to_all | solution.py:109
  210.5 2.0 multiply_reduce_fusion
  213.5 33.0 %scatter_custom_fusion = bf16[4096,1024]{1,0:T(8,128)(2,1)} fusion(s32[2048]{0:T(1024)S(1)} %bitcast.205, bf16[256,1024]{1,0:T(8,128)(2,1)} %multiply_convert_fusion, s32[2048]{0:T(1024)S(1)} %broadcast_clamp_fusion.1, bf16[]{:T(256)} %constant.114.clone.1), kind=kCustom, calls=%fused_computation.49 | custom fusion | bytes 8389120 | tf_op jit(solution)/shard_map/scatter | solution.py:135
  246.4 6.4 all-to-all-start.4
  253.5 2.6 select_bitcast_fusion
  256.1 3.3 copy.96
  259.4 5.2 gather_fusion.2
  264.6 170.4 %all-to-all-done.4 = bf16[16,256,1024]{2,1,0:T(8,128)(2,1)} async-done(((bf16[16,256,1024]{2,1,0:T(8,128)(2,1)}), bf16[16,256,1024]{2,1,0:T(8,128)(2,1)}, u32[]{:S(2)}, u32[]{:S(2)}) %all-to-all-start.4) | async-done | bytes 8388640 | tf_op jit(solution)/shard_map/all_to_all | solution.py:139
  435.0 4.9 all-to-all-start.7
  440.6 46.2 %all-gather.2.cloned.1.call-done = bf16[1,3,1024,512]{3,2,1,0:T(8,128)(2,1)} async-done(((bf16[1,3,1024,256]{3,2,1,0:T(8,128)(2,1)}), bf16[1,3,1024,512]{3,2,1,0:T(8,128)(2,1)}) %all-gather.2.cloned.1.call-update) | async-done | bytes 3145744 | tf_op jit(solution)/shard_map/all_gather | solution.py:138
  486.8 11.4 %fusion.38 = f32[16,256,512]{2,1,0:T(8,128)} fusion(bf16[16,256,1024]{2,1,0:T(8,128)(2,1)} %all-to-all-done.4, bf16[1,3,1024,512]{3,2,1,0:T(8,128)(2,1)} %all-gather.2.cloned.1.call-done), kind=kOutput, calls=%fused_computation.58 | convolution fusion | flops 4294967296 | bytes 17825792 | tf_op jit(solution)/shard_map/sejd,edf->sejf/dot_general | solution.py:142
  498.2 16.0 %convolution_convert_fusion = bf16[16,256,1024]{2,1,0:T(8,128)(2,1)} fusion(f32[16,256,512]{2,1,0:T(8,128)} %fusion.38, bf16[16,256,1024]{2,1,0:T(8,128)(2,1)} %all-to-all-done.4, bf16[1,3,1024,512]{3,2,1,0:T(8,128)(2,1)} %all-gather.2.cloned.1.call-done), kind=kOutput, calls=%fused_computation.47 | convolution fusion | flops 8606711808 | bytes 27262976 | tf_op jit(solution)/shard_map/sejf,edf->sejd/dot_general | solution.py:149
  514.2 18.2 %all-to-all-done.7 = bf16[16,16,4,16,128]{4,3,2,1,0:T(8,128)(2,1)} async-done(((bf16[16,16,4,16,128]{4,3,2,1,0:T(8,128)(2,1)}), bf16[16,16,4,16,128]{4,3,2,1,0:T(8,128)(2,1)}, u32[]{:S(2)}, u32[]{:S(2)}) %all-to-all-start.7) | async-done | bytes 4194336 | tf_op jit(solution)/shard_map/all_to_all | solution.py:108
  532.4 5.3 all-to-all-start.5
  539.1 3.1 broadcast_in_dim.106
  542.2 33.5 %scatter_fusion = bf16[256,4,16,128]{3,2,1,0:T(8,128)(2,1)} fusion(bf16[256,4,16,128]{3,2,1,0:T(8,128)(2,1)} %broadcast_in_dim.106, s32[256]{0:T(256)S(1)} %bitcast.209, bf16[256,4,16,128]{3,2,1,0:T(8,128)(2,1)} %bitcast.57), kind=kCustom, calls=%fused_computation.5 | custom fusion | bytes 12583936 | tf_op jit(solution)/shard_map/scatter | solution.py:116
  575.7 144.2 %all-to-all-done.5 = bf16[16,256,1024]{2,1,0:T(8,128)(2,1)} async-done(((bf16[16,256,1024]{2,1,0:T(8,128)(2,1)}), bf16[16,256,1024]{2,1,0:T(8,128)(2,1)}, u32[]{:S(2)}, u32[]{:S(2)}) %all-to-all-start.5) | async-done | bytes 8388640 | tf_op jit(solution)/shard_map/all_to_all | solution.py:152
  719.9 15.5 %gather_fusion = bf16[2048,1024]{1,0:T(8,128)(2,1)} fusion(bf16[4096,1024]{1,0:T(8,128)(2,1)} %bitcast.46, s32[2048]{0:T(1024)S(1)} %broadcast_clamp_fusion), kind=kCustom, calls=%fused_computation.1 | custom fusion | bytes 8396800 | tf_op jit(solution)/shard_map/gather | solution.py:155
  735.3 4.8 fusion.26
  (89 shorter events, 28.1 us)
Async XLA Ops:
  7.2 203.3 %copy-start = (bf16[1024,1024]{1,0:T(8,128)(2,1)S(1)}, bf16[1024,1024]{1,0:T(8,128)(2,1)}, u32[]{:S(2)}) copy-start(bf16[1024,1024]{1,0:T(8,128)(2,1)} %param.20) | copy-start | bytes 6291460
  7.2 16.5 %copy-start.4 = (s32[256,8]{0,1:T(8,128)S(1)}, s32[256,8]{0,1:T(8,128)}, u32[]{:S(2)}) copy-start(s32[256,8]{0,1:T(8,128)} %param.22) | copy-start | bytes 24580
  9.3 10.9 %all-to-all-start.1 = ((bf16[2,128,8,128]{3,1,0,2:T(8,128)(2,1)}), bf16[2,128,8,128]{3,1,0,2:T(8,128)(2,1)S(1)}, u32[]{:S(2)}, u32[]{:S(2)}) async-start(bf16[2,128,8,128]{3,1,0,2:T(8,128)(2,1)} %copy.81), calls=%async_computation.1 | async-start | bytes 1048576 | tf_op jit(solution)/shard_map/all_to_all | solution.py:89
  20.1 9.9 %all-to-all-start.2 = ((bf16[2,128,8,128]{1,3,0,2:T(8,128)(2,1)}), bf16[2,128,8,128]{1,3,0,2:T(8,128)(2,1)S(1)}, u32[]{:S(2)}, u32[]{:S(2)}) async-start(bf16[2,128,8,128]{1,3,0,2:T(8,128)(2,1)} %copy.84), calls=%async_computation.2 | async-start | bytes 1048576 | tf_op jit(solution)/shard_map/all_to_all | solution.py:90
  29.0 12.1 %copy-start.10 = (s32[32]{0:T(128)S(1)}, s32[32]{0:T(128)}, u32[]{:S(2)}) copy-start(s32[32]{0:T(128)} %param.18) | copy-start | bytes 388
  29.0 12.2 %copy-start.9 = (s32[2,128]{1,0:T(2,128)S(1)}, s32[2,128]{1,0:T(2,128)}, u32[]{:S(2)}) copy-start(s32[2,128]{1,0:T(2,128)} %param.25) | copy-start | bytes 3076
  29.0 16.0 %copy-start.11 = (s32[32]{0:T(128)S(1)}, s32[32]{0:T(128)}, u32[]{:S(2)}) copy-start(s32[32]{0:T(128)} %param.19) | copy-start | bytes 388
  30.1 50.6 %all-to-all-start = ((bf16[2,1024,8,128]{3,1,0,2:T(8,128)(2,1)}), bf16[2,1024,8,128]{3,1,0,2:T(8,128)(2,1)}, u32[]{:S(2)}, u32[]{:S(2)}) async-start(bf16[2,1024,8,128]{3,1,0,2:T(8,128)(2,1)} %copy.78), calls=%async_computation | async-start | bytes 8388608 | tf_op jit(solution)/shard_map/all_to_all | solution.py:88
  85.3 107.8 %copy-start.8 = (s32[256]{0:T(256)S(1)}, s32[256]{0:T(256)}, u32[]{:S(2)}) copy-start(s32[256]{0:T(256)} %compare_select_fusion.3) | copy-start | bytes 3076
  85.3 107.8 %copy-start.1 = (s32[256]{0:T(256)S(1)}, s32[256]{0:T(256)}, u32[]{:S(2)}) copy-start(s32[256]{0:T(256)} %get-tuple-element.133) | copy-start | bytes 3076
  92.3 2.8 copy-start.2
  92.3 3.5 copy-start.3
  144.4 2.8 copy-start.2
  144.4 3.5 copy-start.3
  189.4 23.1 %copy-start.7 = (f32[1024]{0:T(1024)S(1)}, f32[1024]{0:T(1024)}, u32[]{:S(2)}) copy-start(f32[1024]{0:T(1024)} %param.21) | copy-start | bytes 12292
  189.4 9.0 %all-to-all-start.3 = ((bf16[2,256,4,128]{3,2,0,1:T(4,128)(2,1)}), bf16[2,256,4,128]{3,2,0,1:T(4,128)(2,1)S(1)}, u32[]{:S(2)}, u32[]{:S(2)}) async-start(bf16[2,256,4,128]{3,2,0,1:T(4,128)(2,1)} %get-tuple-element.80), calls=%async_computation.3 | async-start | bytes 1048576 | tf_op jit(solution)/shard_map/all_to_all | solution.py:93
  195.0 18.4 %copy-start.5 = (s32[2048,1]{0,1:T(1,128)S(1)}, s32[2048,1]{0,1:T(1,128)}, u32[]{:S(2)}) copy-start(s32[2048,1]{0,1:T(1,128)} %compare_select_fusion.1) | copy-start | bytes 24580
  198.4 48.0 %all-to-all-start.6 = ((s32[16,1,16]{2,1,0:T(1,128)}), s32[16,1,16]{2,1,0:T(1,128)S(1)}, u32[]{:S(2)}, u32[]{:S(2)}) async-start(s32[16,1,16]{2,1,0:T(1,128)} %all_to_all.84), calls=%async_computation.6 | async-start | bytes 16384 | tf_op jit(solution)/shard_map/all_to_all | solution.py:109
  246.4 188.6 %all-to-all-start.4 = ((bf16[16,256,1024]{2,1,0:T(8,128)(2,1)}), bf16[16,256,1024]{2,1,0:T(8,128)(2,1)}, u32[]{:S(2)}, u32[]{:S(2)}) async-start(bf16[16,256,1024]{2,1,0:T(8,128)(2,1)} %bitcast.189), calls=%async_computation.4 | async-start | bytes 16777216 | tf_op jit(solution)/shard_map/all_to_all | solution.py:139
  435.0 97.4 %all-to-all-start.7 = ((bf16[16,16,4,16,128]{4,3,2,1,0:T(8,128)(2,1)}), bf16[16,16,4,16,128]{4,3,2,1,0:T(8,128)(2,1)}, u32[]{:S(2)}, u32[]{:S(2)}) async-start(bf16[16,16,4,16,128]{4,3,2,1,0:T(8,128)(2,1)} %bitcast.192), calls=%async_computation.7 | async-start | bytes 8388608 | tf_op jit(solution)/shard_map/all_to_all | solution.py:108
  439.9 46.9 %all-gather.2.cloned.1.call-start = ((), (), s32[]{:S(2)}) async-start(), calls=%async_computation.8 | async-start | bytes 4718592 | tf_op jit(solution)/shard_map/all_gather | solution.py:138
  514.2 23.5 %copy-start.6 = (f32[256,8]{0,1:T(8,128)S(1)}, f32[256,8]{0,1:T(8,128)}, u32[]{:S(2)}) copy-start(f32[256,8]{0,1:T(8,128)} %param.23) | copy-start | bytes 24580
  532.4 187.5 %all-to-all-start.5 = ((bf16[16,256,1024]{2,1,0:T(8,128)(2,1)}), bf16[16,256,1024]{2,1,0:T(8,128)(2,1)}, u32[]{:S(2)}, u32[]{:S(2)}) async-start(bf16[16,256,1024]{2,1,0:T(8,128)(2,1)} %convolution_convert_fusion), calls=%async_computation.5 | async-start | bytes 16777216 | tf_op jit(solution)/shard_map/all_to_all | solution.py:152
Sparse Core Ops, SparseCore 0:
  442.3 44.5 all-gather.1
where the time goes:
time: 760 us; the launch traced here: 748 us
  waiting for transfers between devices  417 us (55%)
  local copies, waits for them, and re-layouts  147 us (19%)
  other arithmetic  68.1 us (9%)
  matrix products  58.8 us (8%)
  starting transfers between devices  43.5 us (6%)
  between operations  14.8 us (2%)
    all_to_all x1, waiting for transfers between devices, body(): lax.all_to_all(buffer, 'req', split_axis=0, concat_axis=0, tiled=True)  170 us
    all_to_all x1, waiting for transfers between devices, body(): lax.all_to_all(expert_out.reshape(slot_block.shape), 'req', split_axis=0,...  144 us
    all_gather x1, waiting for transfers between devices, body(): full_weights = lax.all_gather(w_experts, 'kv', axis=3, tiled=True)  46.2 us
    sub x2, other arithmetic, soft_weights(): probability = jnp.where(allowed, jnp.exp(masked - row_max), 0.0)  38.9 us
    scatter x1, local copies, waits for them, and re-layouts, body(): decode_pool = jnp.zeros((slots_dev, group_count, BLOCK, head_pair), jnp.b...  33.5 us
    scatter x1, local copies, waits for them, and re-layouts, body(): buffer = jnp.zeros((experts * capacity, width_model), jnp.bfloat16).at[ta...  33 us
    all_to_all x1, waiting for transfers between devices, body(): lax.all_to_all(cache, 'kv', split_axis=2, concat_axis=1, tiled=True)  28.7 us
    dynamic_slice x10, local copies, waits for them, and re-layouts, body(): lax.map(whole_request, (query_heads, cache_heads, span_heads, lengths))  20.2 us
  transfers between devices with their start and end apart: 9, of which 8 were waited for; matrix products, arithmetic and copies ran while one was open for 19% of the time, Pallas kernels for 0%

commit v1 on v0

--- a/solution.py
+++ b/solution.py
@@ -5,6 +5,20 @@
 from jax.sharding import PartitionSpec as P
 
 BLOCK = 16
+
+
+def extend_results_in(frame_in, a_name):
+    value_now, prior = (lax.axis_size(a_name), lax.axis_index(a_name))
+    next_value, view_out = (frame_in, 1)
+    while view_out < value_now:
+        left_arr = lax.ppermute(
+            next_value, a_name, [(pp, pp ^ view_out) for pp in range(value_now)]
+        )
+        v_next = jnp.concatenate([next_value, left_arr], axis=3)
+        carry_out = jnp.concatenate([left_arr, next_value], 3)
+        next_value = jnp.where(prior & view_out == 0, v_next, carry_out)
+        view_out = 2 * view_out
+    return next_value
 
 
 def lookup_lengths(req_order, cached_len, count):
@@ -135,7 +149,7 @@
         .set(normed[source_row])
         .reshape(experts, capacity, width_model)
     )
-    full_weights = lax.all_gather(w_experts, "kv", axis=3, tiled=True)
+    full_weights = extend_results_in(w_experts, "kv")
     slot_block = lax.all_to_all(buffer, "req", split_axis=0, concat_axis=0, tiled=True)
     source_count = slot_block.shape[0] // exp_dev
     grouped = slot_block.reshape(source_count, exp_dev, slot_block.shape[1], width_model)

time: 760 us -> 760 us (level)
  local copies, waits for them, and re-layouts: 147 us -> 164 us
  between operations: 14.8 us -> 1.18 us
    all_gather x1 -> x0, waiting for transfers between devices: 46.2 us -> none  [body(): full_weights = lax.all_gather(w_experts, 'kv', axis=3, tiled=True)]
    ppermute x0 -> x1, waiting for transfers between devices: none -> 35.9 us  [extend_results_in(): lax.ppermute(next_value, a_name, [(pp, pp ^ view_out) for pp in range(val...]
    all_to_all x0 -> x1, local copies, waits for them, and re-layouts: none -> 12.3 us  [body(): lax.all_to_all(expert_out.reshape(slot_block.shape), 'req', split_axis=0,...]
where the time goes in v1:
time: 760 us; the launch traced here: 748 us
  waiting for transfers between devices  410 us (54%)
  local copies, waits for them, and re-layouts  164 us (22%)
  other arithmetic  71.7 us (9%)
  matrix products  57 us (8%)
  starting transfers between devices  43.7 us (6%)
    all_to_all x1, waiting for transfers between devices, body(): lax.all_to_all(buffer, 'req', split_axis=0, concat_axis=0, tiled=True)  170 us
    all_to_all x1, waiting for transfers between devices, body(): lax.all_to_all(expert_out.reshape(slot_block.shape), 'req', split_axis=0,...  144 us
    sub x2, other arithmetic, soft_weights(): probability = jnp.where(allowed, jnp.exp(masked - row_max), 0.0)  38.9 us
    ppermute x1, waiting for transfers between devices, extend_results_in(): lax.ppermute(next_value, a_name, [(pp, pp ^ view_out) for pp in range(val...  35.9 us
    scatter x1, local copies, waits for them, and re-layouts, body(): buffer = jnp.zeros((experts * capacity, width_model), jnp.bfloat16).at[ta...  33.9 us
    scatter x1, local copies, waits for them, and re-layouts, body(): decode_pool = jnp.zeros((slots_dev, group_count, BLOCK, head_pair), jnp.b...  33.5 us
    all_to_all x1, waiting for transfers between devices, body(): lax.all_to_all(cache, 'kv', split_axis=2, concat_axis=1, tiled=True)  28.7 us
    all_to_all x1, waiting for transfers between devices, body(): lax.all_to_all(outgoing, 'req', split_axis=0, concat_axis=0, tiled=True)  23 us
  transfers between devices with their start and end apart: 9, of which 8 were waited for; matrix products, arithmetic and copies ran while one was open for 19% of the time, Pallas kernels for 0%

profile of v1, /device:TPU:11, one launch (start us, length us, event | category | flops | bytes accessed | tf_op | source)
XLA Modules:
  0.0 748.2 jit_solution(6504406986900866038)
XLA Ops:
  0.7 2.1 copy.110
  2.7 3.5 all-to-all-start.1
  8.4 5.2 all-to-all-done.1
  13.6 3.5 all-to-all-start.2
  17.5 5.0 copy.107
  23.6 5.6 all-to-all-start
  29.2 4.5 reduce-window.6
  35.3 3.2 sort.17
  42.3 2.2 all_to_all.74
  45.5 28.7 %all-to-all-done = bf16[2,1024,8,128]{3,1,0,2:T(8,128)(2,1)} async-done(((bf16[2,1024,8,128]{3,1,0,2:T(8,128)(2,1)}), bf16[2,1024,8,128]{3,1,0,2:T(8,128)(2,1)}, u32[]{:S(2)}, u32[]{:S(2)}) %all-to-all-start) | async-done | bytes 4194336 | tf_op jit(solution)/shard_map/all_to_all | solution.py:102
  74.1 4.6 copy.109
  78.7 104.1 %while.12 = (s32[]{:T(128)}, bf16[2,256,4,128]{3,2,0,1:T(4,128)(2,1)}, bf16[2,2048,4,128]{3,1,2,0:T(8,128)(2,1)}, bf16[2,256,4,128]{1,3,2,0:T(8,128)(2,1)}, s32[...) while((s32[]{:T(128)}, bf16[2,256,4,128]{3,2,0,1:T(4,128)(2,1)}, ...), condition=%wide.region_4.5_spmd, body=%wide.region_1.4_spmd.sunk | while | flops 1251877888 | bytes 80653984 | solution.py:106
  78.7 3.0 constant_dynamic-slice_fusion.5
  81.8 4.0 copy.153
  85.8 2.8 fusion.64
  91.1 9.2 %fusion.65 = f32[4,2304,256,2]{2,1,3,0:T(8,128)} fusion(bf16[256,4,2,64]{0,3,2,1:T(8,128)(2,1)S(1)} %bitcast.193, bf16[256,4,64]{0,2,1:T(8,128)(2,1)} %get-tuple-element.183, bf16[2048,4,64]{0,2,1:T(8,128)(2,1)} %get-tuple-element.184), kind=kOutput, calls=%fused_computation.24.clone.1 | convolution fusion | flops 606339072 | bytes 20316160 | tf_op jit(solution)/shard_map/while/body/eval_jaxpr/igsd,pgd->gsip/dot_general | solution.py:38
  102.2 2.7 fusion.66
  104.9 19.4 %fusion.67 = (f32[4,2,256]{2,1,0:T(2,128)S(1)}, bf16[4,2,256,2304]{2,3,1,0:T(8,128)(2,1)}) fusion(f32[4,2304,256,2]{2,1,3,0:T(8,128)} %fusion.65, pred[256,2304]{0,1:T(8,128)(4,1)} %fusion.66), kind=kOutput, calls=%fused_computation.100.clone.1 | output fusion | flops 37751040 | bytes 28909568 | tf_op jit(solution)/shard_map/while/body/eval_jaxpr/sub | solution.py:47
  124.3 5.5 fusion.68
  130.8 3.0 constant_dynamic-slice_fusion.5
  133.8 4.0 copy.153
  137.8 2.8 fusion.64
  143.2 9.2 %fusion.65 = f32[4,2304,256,2]{2,1,3,0:T(8,128)} fusion(bf16[256,4,2,64]{0,3,2,1:T(8,128)(2,1)S(1)} %bitcast.193, bf16[256,4,64]{0,2,1:T(8,128)(2,1)} %get-tuple-element.183, bf16[2048,4,64]{0,2,1:T(8,128)(2,1)} %get-tuple-element.184), kind=kOutput, calls=%fused_computation.24.clone.1 | convolution fusion | flops 606339072 | bytes 20316160 | tf_op jit(solution)/shard_map/while/body/eval_jaxpr/igsd,pgd->gsip/dot_general | solution.py:38
  154.3 2.7 fusion.66
  157.0 19.4 %fusion.67 = (f32[4,2,256]{2,1,0:T(2,128)S(1)}, bf16[4,2,256,2304]{2,3,1,0:T(8,128)(2,1)}) fusion(f32[4,2304,256,2]{2,1,3,0:T(8,128)} %fusion.65, pred[256,2304]{0,1:T(8,128)(4,1)} %fusion.66), kind=kOutput, calls=%fused_computation.100.clone.1 | output fusion | flops 37751040 | bytes 28909568 | tf_op jit(solution)/shard_map/while/body/eval_jaxpr/sub | solution.py:47
  176.4 5.5 fusion.68
  182.9 3.6 all-to-all-start.3
  191.9 11.0 %all-to-all-start.6 = ((s32[16,1,16]{2,1,0:T(1,128)}), s32[16,1,16]{2,1,0:T(1,128)S(1)}, u32[]{:S(2)}, u32[]{:S(2)}) async-start(s32[16,1,16]{2,1,0:T(1,128)} %all_to_all.84), calls=%async_computation.6 | async-start | bytes 16384 | tf_op jit(solution)/shard_map/all_to_all | solution.py:123
  207.2 33.9 %scatter_custom_fusion = bf16[4096,1024]{1,0:T(8,128)(2,1)} fusion(s32[2048]{0:T(1024)S(1)} %bitcast.208, bf16[256,1024]{1,0:T(8,128)(2,1)} %multiply_convert_fusion, s32[2048]{0:T(1024)S(1)} %broadcast_clamp_fusion.1, bf16[]{:T(256)} %constant.117.clone.1), kind=kCustom, calls=%fused_computation.49 | custom fusion | bytes 8389120 | tf_op jit(solution)/shard_map/scatter | solution.py:149
  241.1 6.3 all-to-all-start.4
  248.2 2.6 select_bitcast_fusion
  250.8 3.3 copy.131
  254.1 5.2 gather_fusion.2
  259.3 170.4 %all-to-all-done.4 = bf16[16,256,1024]{2,1,0:T(8,128)(2,1)} async-done(((bf16[16,256,1024]{2,1,0:T(8,128)(2,1)}), bf16[16,256,1024]{2,1,0:T(8,128)(2,1)}, u32[]{:S(2)}, u32[]{:S(2)}) %all-to-all-start.4) | async-done | bytes 8388640 | tf_op jit(solution)/shard_map/all_to_all | solution.py:153
  429.7 4.9 all-to-all-start.7
  434.6 2.6 copy.122
  437.1 35.9 %collective-permute-done = bf16[1,3,1024,256]{2,3,1,0:T(8,128)(2,1)} collective-permute-done((bf16[1,3,1024,256]{2,3,1,0:T(8,128)(2,1)}, bf16[1,3,1024,256]{2,3,1,0:T(8,128)(2,1)}, u32[]{:S(2)}, u32[]{:S(2)}) %collective-permute-start) | collective-permute-done | bytes 1572896 | tf_op jit(solution)/shard_map/ppermute | solution.py:14
  473.1 3.6 maximum_select_fusion
  478.4 10.1 %fusion.38 = f32[512,16,256]{2,0,1:T(8,128)} fusion(bf16[16,256,1024]{2,1,0:T(8,128)(2,1)} %all-to-all-done.4, bf16[1,3,1024,512]{2,3,1,0:T(8,128)(2,1)S(1)} %maximum_select_fusion), kind=kOutput, calls=%fused_computation.58 | convolution fusion | flops 4294967296 | bytes 17825792 | tf_op jit(solution)/shard_map/sejd,edf->sejf/dot_general | solution.py:156
  488.5 15.5 %convert_bitcast_fusion = bf16[16,256,1024]{1,2,0:T(8,128)(2,1)} fusion(f32[512,16,256]{2,0,1:T(8,128)} %fusion.38, bf16[16,256,1024]{2,1,0:T(8,128)(2,1)} %all-to-all-done.4, bf16[1,3,1024,512]{2,3,1,0:T(8,128)(2,1)} %copy-done.4), kind=kOutput, calls=%fused_computation.47 | convolution fusion | flops 8606711808 | bytes 27262976 | tf_op jit(solution)/shard_map/sejf,edf->sejd/dot_general | solution.py:163
  504.0 23.0 %all-to-all-done.7 = bf16[16,16,4,16,128]{4,3,2,1,0:T(8,128)(2,1)} async-done(((bf16[16,16,4,16,128]{4,3,2,1,0:T(8,128)(2,1)}), bf16[16,16,4,16,128]{4,3,2,1,0:T(8,128)(2,1)}, u32[]{:S(2)}, u32[]{:S(2)}) %all-to-all-start.7) | async-done | bytes 4194336 | tf_op jit(solution)/shard_map/all_to_all | solution.py:122
  527.0 5.3 all-to-all-start.5
  533.7 3.1 broadcast_in_dim.106
  536.8 33.5 %scatter_fusion = bf16[256,4,16,128]{3,2,1,0:T(8,128)(2,1)} fusion(bf16[256,4,16,128]{3,2,1,0:T(8,128)(2,1)} %broadcast_in_dim.106, s32[256]{0:T(256)S(1)} %bitcast.212, bf16[256,4,16,128]{3,2,1,0:T(8,128)(2,1)} %bitcast.57), kind=kCustom, calls=%fused_computation.5 | custom fusion | bytes 12583936 | tf_op jit(solution)/shard_map/scatter | solution.py:130
  570.3 144.2 %all-to-all-done.5 = bf16[16,256,1024]{1,2,0:T(8,128)(2,1)} async-done(((bf16[16,256,1024]{1,2,0:T(8,128)(2,1)}), bf16[16,256,1024]{1,2,0:T(8,128)(2,1)}, u32[]{:S(2)}, u32[]{:S(2)}) %all-to-all-start.5) | async-done | bytes 8388640 | tf_op jit(solution)/shard_map/all_to_all | solution.py:166
  714.5 12.3 %copy.129 = bf16[16,256,1024]{2,1,0:T(8,128)(2,1)} copy(bf16[16,256,1024]{1,2,0:T(8,128)(2,1)} %all-to-all-done.5) | data formatting | bytes 16777216 | tf_op jit(solution)/shard_map/all_to_all | solution.py:166
  726.8 15.4 %gather_fusion = bf16[2048,1024]{1,0:T(8,128)(2,1)} fusion(bf16[4096,1024]{1,0:T(8,128)(2,1)} %bitcast.188, s32[2048]{0:T(1024)S(1)} %broadcast_clamp_fusion), kind=kCustom, calls=%fused_computation.1 | custom fusion | bytes 8396800 | tf_op jit(solution)/shard_map/gather | solution.py:169
  742.2 4.8 fusion.26
  (93 shorter events, 35.0 us)
Async XLA Ops:
  0.6 203.6 %copy-start = (bf16[1024,1024]{1,0:T(8,128)(2,1)S(1)}, bf16[1024,1024]{1,0:T(8,128)(2,1)}, u32[]{:S(2)}) copy-start(bf16[1024,1024]{1,0:T(8,128)(2,1)} %param.20) | copy-start | bytes 6291460
  0.6 16.5 %copy-start.5 = (s32[256,8]{0,1:T(8,128)S(1)}, s32[256,8]{0,1:T(8,128)}, u32[]{:S(2)}) copy-start(s32[256,8]{0,1:T(8,128)} %param.22) | copy-start | bytes 24580
  2.7 10.9 %all-to-all-start.1 = ((bf16[2,128,8,128]{3,1,0,2:T(8,128)(2,1)}), bf16[2,128,8,128]{3,1,0,2:T(8,128)(2,1)S(1)}, u32[]{:S(2)}, u32[]{:S(2)}) async-start(bf16[2,128,8,128]{3,1,0,2:T(8,128)(2,1)} %copy.110), calls=%async_computation.1 | async-start | bytes 1048576 | tf_op jit(solution)/shard_map/all_to_all | solution.py:103
  13.6 9.9 %all-to-all-start.2 = ((bf16[2,128,8,128]{1,3,0,2:T(8,128)(2,1)}), bf16[2,128,8,128]{1,3,0,2:T(8,128)(2,1)S(1)}, u32[]{:S(2)}, u32[]{:S(2)}) async-start(bf16[2,128,8,128]{1,3,0,2:T(8,128)(2,1)} %copy.113), calls=%async_computation.2 | async-start | bytes 1048576 | tf_op jit(solution)/shard_map/all_to_all | solution.py:104
  22.5 12.1 %copy-start.11 = (s32[32]{0:T(128)S(1)}, s32[32]{0:T(128)}, u32[]{:S(2)}) copy-start(s32[32]{0:T(128)} %param.18) | copy-start | bytes 388
  22.5 12.2 %copy-start.10 = (s32[2,128]{1,0:T(2,128)S(1)}, s32[2,128]{1,0:T(2,128)}, u32[]{:S(2)}) copy-start(s32[2,128]{1,0:T(2,128)} %param.25) | copy-start | bytes 3076
  22.5 16.0 %copy-start.12 = (s32[32]{0:T(128)S(1)}, s32[32]{0:T(128)}, u32[]{:S(2)}) copy-start(s32[32]{0:T(128)} %param.19) | copy-start | bytes 388
  23.6 50.6 %all-to-all-start = ((bf16[2,1024,8,128]{3,1,0,2:T(8,128)(2,1)}), bf16[2,1024,8,128]{3,1,0,2:T(8,128)(2,1)}, u32[]{:S(2)}, u32[]{:S(2)}) async-start(bf16[2,1024,8,128]{3,1,0,2:T(8,128)(2,1)} %copy.107), calls=%async_computation | async-start | bytes 8388608 | tf_op jit(solution)/shard_map/all_to_all | solution.py:102
  78.7 107.8 %copy-start.9 = (s32[256]{0:T(256)S(1)}, s32[256]{0:T(256)}, u32[]{:S(2)}) copy-start(s32[256]{0:T(256)} %compare_select_fusion.3) | copy-start | bytes 3076
  78.7 107.8 %copy-start.1 = (s32[256]{0:T(256)S(1)}, s32[256]{0:T(256)}, u32[]{:S(2)}) copy-start(s32[256]{0:T(256)} %get-tuple-element.133) | copy-start | bytes 3076
  85.8 2.8 copy-start.2
  85.8 3.5 copy-start.3
  137.8 2.8 copy-start.2
  137.8 3.5 copy-start.3
  182.9 23.4 %copy-start.8 = (f32[1024]{0:T(1024)S(1)}, f32[1024]{0:T(1024)}, u32[]{:S(2)}) copy-start(f32[1024]{0:T(1024)} %param.21) | copy-start | bytes 12292
  182.9 9.0 %all-to-all-start.3 = ((bf16[2,256,4,128]{3,2,0,1:T(4,128)(2,1)}), bf16[2,256,4,128]{3,2,0,1:T(4,128)(2,1)S(1)}, u32[]{:S(2)}, u32[]{:S(2)}) async-start(bf16[2,256,4,128]{3,2,0,1:T(4,128)(2,1)} %get-tuple-element.80), calls=%async_computation.3 | async-start | bytes 1048576 | tf_op jit(solution)/shard_map/all_to_all | solution.py:107
  188.5 18.7 %copy-start.6 = (s32[2048,1]{0,1:T(1,128)S(1)}, s32[2048,1]{0,1:T(1,128)}, u32[]{:S(2)}) copy-start(s32[2048,1]{0,1:T(1,128)} %compare_select_fusion.1) | copy-start | bytes 24580
  191.9 49.2 %all-to-all-start.6 = ((s32[16,1,16]{2,1,0:T(1,128)}), s32[16,1,16]{2,1,0:T(1,128)S(1)}, u32[]{:S(2)}, u32[]{:S(2)}) async-start(s32[16,1,16]{2,1,0:T(1,128)} %all_to_all.84), calls=%async_computation.6 | async-start | bytes 16384 | tf_op jit(solution)/shard_map/all_to_all | solution.py:123
  241.1 188.5 %all-to-all-start.4 = ((bf16[16,256,1024]{2,1,0:T(8,128)(2,1)}), bf16[16,256,1024]{2,1,0:T(8,128)(2,1)}, u32[]{:S(2)}, u32[]{:S(2)}) async-start(bf16[16,256,1024]{2,1,0:T(8,128)(2,1)} %bitcast.192), calls=%async_computation.4 | async-start | bytes 16777216 | tf_op jit(solution)/shard_map/all_to_all | solution.py:153
  429.7 97.4 %all-to-all-start.7 = ((bf16[16,16,4,16,128]{4,3,2,1,0:T(8,128)(2,1)}), bf16[16,16,4,16,128]{4,3,2,1,0:T(8,128)(2,1)}, u32[]{:S(2)}, u32[]{:S(2)}) async-start(bf16[16,16,4,16,128]{4,3,2,1,0:T(8,128)(2,1)} %bitcast.195), calls=%async_computation.7 | async-start | bytes 8388608 | tf_op jit(solution)/shard_map/all_to_all | solution.py:122
  437.1 35.9 %collective-permute-start = (bf16[1,3,1024,256]{2,3,1,0:T(8,128)(2,1)}, bf16[1,3,1024,256]{2,3,1,0:T(8,128)(2,1)}, u32[]{:S(2)}, u32[]{:S(2)}) collective-permute-start(bf16[1,3,1024,256]{2,3,1,0:T(8,128)(2,1)} %copy.122), channel_id=1, source_target_pairs={{0,1},{1,0},{2,3},{3,2},{4,5},{5,4},{6,7},{7,6},{8,9},{9,8},{10,11... | collective-permute-start | bytes 4718600 | tf_op jit(solution)/shard_map/ppermute | solution.py:14
  476.7 1.7 copy-start.4
  504.0 28.3 %copy-start.7 = (f32[256,8]{0,1:T(8,128)S(1)}, f32[256,8]{0,1:T(8,128)}, u32[]{:S(2)}) copy-start(f32[256,8]{0,1:T(8,128)} %param.23) | copy-start | bytes 24580
  527.0 187.5 %all-to-all-start.5 = ((bf16[16,256,1024]{1,2,0:T(8,128)(2,1)}), bf16[16,256,1024]{1,2,0:T(8,128)(2,1)}, u32[]{:S(2)}, u32[]{:S(2)}) async-start(bf16[16,256,1024]{1,2,0:T(8,128)(2,1)} %convert_bitcast_fusion), calls=%async_computation.5 | async-start | bytes 16777216 | tf_op jit(solution)/shard_map/all_to_all | solution.py:166
